TPU v7x, 32 devices: a whole 2x2x4 slice. The times are simulated.
32 devices in a mesh: strip: 8 (over z, x), chan: 4 (over y, core).
Axes of the slice: x: 2, y: 2, z: 4, core: 2. Of those that a mesh axis runs over, the one named last changes fastest.
Arguments:
- features: bfloat16 [512, 32, 128], P('chan', 'strip'), may hold values from -6 to 6
- first_filters: bfloat16 [512, 3, 3, 512], P('chan'), may hold values from -0.09375 to 0.09375
- second_filters: bfloat16 [512, 3, 3, 512], P('chan'), may hold values from -0.09375 to 0.09375
- out_grad: bfloat16 [512, 32, 128], P('chan', 'strip'), may hold values from -6 to 6
Outputs:
- output: bfloat16 [512, 32, 128], P('chan', 'strip')
- input_grad: bfloat16 [512, 32, 128], P('chan', 'strip')
- first_grad: float32 [512, 3, 3, 512], P('chan')
- second_grad: float32 [512, 3, 3, 512], P('chan')
All inputs are finite; a program needn't handle non-finite values.
Results may differ from a plain program's by a relative error of at most 0.005.
Values may be sent and summed in bfloat16 or wider, within the bound.
No kernel may reach another device: no remote copies, remote signals or barrier semaphores. Data moves between devices by JAX's collectives and lax.ppermute only.
A program may use at most 128 MiB of HBM per device.

v0:
```python
import jax
import jax.numpy as jnp
from jax import lax
from jax.sharding import PartitionSpec as P


def extended(cells, sides, width):
    for axis, dim in sides:
        count = lax.axis_size(axis)
        ends = count - 1
        head = lax.slice_in_dim(cells, 0, width, axis=dim)
        tail = lax.slice_in_dim(cells, cells.shape[dim] - width, cells.shape[dim], axis=dim)
        cells = jnp.concatenate(
            [
                lax.ppermute(tail, axis, [(i, (i + 1) % count) for i in range(ends)]),
                cells,
                lax.ppermute(head, axis, [((i + 1) % count, i) for i in range(ends)]),
            ],
            axis=dim,
        )
    return cells


def take_cols(field, shift):
    if shift == 0:
        return field
    edge = jnp.zeros(field.shape[:-1] + (1,), field.dtype)
    if shift > 0:
        return jnp.concatenate([field[..., 1:], edge], axis=-1)
    return jnp.concatenate([edge, field[..., :-1]], axis=-1)


def conv_fwd(padded, weight):
    chans, rows_pad, cols = padded.shape
    rows = rows_pad - 2
    outs = weight.shape[0]
    flat_w = weight.reshape(outs * 9, chans)
    taps = jnp.dot(
        flat_w, padded.reshape(chans, rows_pad * cols), preferred_element_type=jnp.float32
    )
    taps = taps.reshape(outs, 3, 3, rows_pad, cols)
    total = jnp.zeros((outs, rows, cols), jnp.float32)
    for kh in range(3):
        for kw in range(3):
            total = total + take_cols(taps[:, kh, kw, kh : kh + rows, :], kw - 1)
    return total


def back_stack(padded):
    outs, rows_pad, cols = padded.shape
    rows = rows_pad - 2
    pieces = []
    for kh in range(3):
        for kw in range(3):
            pieces.append(take_cols(padded[:, 2 - kh : 2 - kh + rows, :], 1 - kw))
    return jnp.stack(pieces, axis=1).reshape(outs * 9, rows * cols)


def conv_back_stacked(stacked, weight, rows, cols):
    outs = weight.shape[0]
    inner = weight.shape[3]
    flat_w = weight.reshape(outs * 9, inner)
    result = lax.dot_general(
        flat_w, stacked, (((0,), (0,)), ((), ())), preferred_element_type=jnp.float32
    )
    return result.reshape(inner, rows, cols)


def filter_grad(grad_out, padded):
    outs, rows, cols = grad_out.shape
    chans, rows_pad, _ = padded.shape
    pieces = []
    for kh in range(3):
        for kw in range(3):
            moved = take_cols(grad_out, 1 - kw)
            pieces.append(jnp.pad(moved, ((0, 0), (kh, 2 - kh), (0, 0))))
    stacked = jnp.stack(pieces, axis=1).reshape(outs * 9, rows_pad * cols)
    result = lax.dot_general(
        stacked,
        padded.reshape(chans, rows_pad * cols),
        (((1,), (1,)), ((), ())),
        preferred_element_type=jnp.float32,
    )
    return result.reshape(outs, 3, 3, chans)


def body(features, first_filters, second_filters, out_grad):
    blocks, rows, cols = features.shape
    x_pad = extended(features, (("strip", 1),), 1)
    x_all = lax.all_gather(x_pad, "chan", axis=0, tiled=True)
    pre_full = conv_fwd(x_all, first_filters)
    pre = pre_full.astype(jnp.bfloat16)
    hidden = jax.nn.silu(pre_full).astype(jnp.bfloat16)
    h_pad = extended(hidden, (("strip", 1),), 1)
    h_all = lax.all_gather(h_pad, "chan", axis=0, tiled=True)
    output = (features.astype(jnp.float32) + conv_fwd(h_all, second_filters)).astype(jnp.bfloat16)
    dy_pad = extended(out_grad, (("strip", 1),), 1)
    second_grad = filter_grad(out_grad, h_all)
    second_grad = lax.psum(second_grad, "strip")
    dy_stack = back_stack(dy_pad)
    hidden_grad = lax.psum_scatter(
        conv_back_stacked(dy_stack, second_filters, rows, cols),
        "chan",
        scatter_dimension=0,
        tiled=True,
    )
    pre_val = pre.astype(jnp.float32)
    sig = jax.nn.sigmoid(pre_val)
    pre_grad = (hidden_grad * sig * (1.0 + pre_val * (1.0 - sig))).astype(jnp.bfloat16)
    da_pad = extended(pre_grad, (("strip", 1),), 1)
    first_grad = filter_grad(pre_grad, x_all)
    da_stack = back_stack(da_pad)
    input_term = lax.psum_scatter(
        conv_back_stacked(da_stack, first_filters, rows, cols),
        "chan",
        scatter_dimension=0,
        tiled=True,
    )
    input_grad = (out_grad.astype(jnp.float32) + input_term).astype(jnp.bfloat16)
    first_grad = lax.psum(first_grad, "strip")
    return (output, input_grad, first_grad, second_grad)


def solution(mesh):
    in_specs = (
        P("chan", "strip", None),
        P("chan", None, None, None),
        P("chan", None, None, None),
        P("chan", "strip", None),
    )
    out_specs = (
        P("chan", "strip", None),
        P("chan", "strip", None),
        P("chan", None, None, None),
        P("chan", None, None, None),
    )
    return jax.shard_map(body, mesh=mesh, in_specs=in_specs, out_specs=out_specs, check_vma=False)
```

profile of v0, /device:TPU:0, one launch (start us, length us, event | category | flops | bytes accessed | tf_op | source)
XLA Modules:
  0.0 330.2 jit_solution(18411592274643033092)
XLA Ops:
  7.2 1.0 copy.99
  8.3 4.8 %collective-permute-start.5 = (bf16[128,1,128]{0,2,1:T(8,128)(2,1)S(1)}, bf16[128,1,128]{0,2,1:T(8,128)(2,1)S(1)}, u32[]{:S(2)}, u32[]{:S(2)}) collective-permute-start(bf16[128,1,128]{0,2,1:T(8,128)(2,1)S(1)} %get-tuple-element.34), channel_id=1, source_target_pairs={{0,4},{4,8},{8,12},{12,16},{16,20},{20,24},{24,28},{1,5},{5,9},{9,... | collective-permute-start | bytes 98312 | tf_op jit(solution)/shard_map/ppermute | solution.py:15
  13.1 1.3 collective-permute-start.4
  14.4 1.0 copy.72
  15.5 1.3 collective-permute-start.1
  16.8 5.2 %collective-permute-start = (bf16[128,1,128]{0,2,1:T(8,128)(2,1)S(1)}, bf16[128,1,128]{0,2,1:T(8,128)(2,1)S(1)}, u32[]{:S(2)}, u32[]{:S(2)}) collective-permute-start(bf16[128,1,128]{0,2,1:T(8,128)(2,1)S(1)} %get-tuple-element.28), channel_id=1, source_target_pairs={{0,4},{4,8},{8,12},{12,16},{16,20},{20,24},{24,28},{1,5},{5,9},{9,... | collective-permute-start | bytes 98312 | tf_op jit(solution)/shard_map/ppermute | solution.py:15
  22.0 2.3 copy.88
  24.3 1.1 reshape.54
  25.3 2.7 copy.75
  28.1 2.2 reshape.51
  30.3 0.6 dynamic-slice
  31.9 2.0 copy.105
  33.9 2.1 fusion.3
  36.1 1.3 copy.106
  37.6 8.8 %all_gather.6 = bf16[512,6,128]{0,2,1:T(8,128)(2,1)S(1)} all-gather(bf16[128,6,128]{0,2,1:T(8,128)(2,1)S(1)} %pad_maximum_fusion.1), channel_id=1, replica_groups=mesh['strip'=8,'chan'=4] {'chan'}, dimensions={0}, use_global_device_ids=true | all-gather | bytes 983040 | tf_op jit(solution)/shard_map/all_gather | solution.py:90
  46.3 3.0 convolution_bitcast_fusion.1
  49.3 5.2 %copy.76 = f32[1152,768]{1,0:T(8,128)} copy(f32[1152,768]{0,1:T(8,128)} %convolution_bitcast_fusion.1) | data formatting | bytes 7077888 | tf_op jit(solution)/shard_map/dot_general | solution.py:38
  54.5 4.8 %reshape.52 = f32[128,3,3,6,128]{4,3,2,1,0:T(8,128)} reshape(f32[1152,768]{1,0:T(8,128)} %copy.76) | data formatting | bytes 7077888 | tf_op jit(solution)/shard_map/reshape | solution.py:41
  59.4 2.3 slice_bitcast_fusion.17
  61.6 0.7 bitcast_dynamic-update-slice_fusion.17
  62.3 0.7 bitcast_dynamic-update-slice_fusion.16
  63.0 0.7 bitcast_dynamic-update-slice_fusion.15
  63.8 0.7 bitcast_dynamic-update-slice_fusion.14
  64.5 0.7 bitcast_dynamic-update-slice_fusion.13
  65.2 0.9 slice.264
  66.1 0.9 slice.259
  67.0 0.9 slice.254
  67.9 0.7 bitcast_dynamic-update-slice_fusion.12
  68.6 0.7 bitcast_dynamic-update-slice_fusion.11
  69.3 0.7 bitcast_dynamic-update-slice_fusion.10
  70.0 0.7 bitcast_dynamic-update-slice_fusion.9
  70.7 4.7 %all-reduce.49.cloned.1.call-done = f32[512,4,128]{2,1,0:T(4,128)} async-done(((f32[512,4,128]{2,1,0:T(4,128)}), f32[512,4,128]{2,1,0:T(4,128)}) %all-reduce.49.cloned.1.call-update) | async-done | bytes 1048592
  75.4 2.3 fusion.11
  78.0 1.3 collective-permute-start.3
  79.3 4.5 %collective-permute-start.2 = (bf16[128,1,128]{2,1,0:T(2,128)(2,1)S(1)}, bf16[128,1,128]{2,1,0:T(2,128)(2,1)S(1)}, u32[]{:S(2)}, u32[]{:S(2)}) collective-permute-start(bf16[128,1,128]{2,1,0:T(2,128)(2,1)S(1)} %get-tuple-element.26), channel_id=1, source_target_pairs={{0,4},{4,8},{8,12},{12,16},{16,20},{20,24},{24,28},{1,5},{5,9},{9,... | collective-permute-start | bytes 98312 | tf_op jit(solution)/shard_map/ppermute | solution.py:15
  83.9 4.3 %collective-permute-start.7 = (bf16[128,1,128]{2,1,0:T(2,128)(2,1)S(1)}, bf16[128,1,128]{2,1,0:T(2,128)(2,1)S(1)}, u32[]{:S(2)}, u32[]{:S(2)}) collective-permute-start(bf16[128,1,128]{2,1,0:T(2,128)(2,1)S(1)} %get-tuple-element.24), channel_id=1, source_target_pairs={{0,4},{4,8},{8,12},{12,16},{16,20},{20,24},{24,28},{1,5},{5,9},{9,... | collective-permute-start | bytes 98312 | tf_op jit(solution)/shard_map/ppermute | solution.py:15
  88.2 1.3 collective-permute-start.6
  89.8 8.7 %all_gather.7 = bf16[512,6,128]{2,0,1:T(8,128)(2,1)} all-gather(bf16[128,6,128]{2,0,1:T(8,128)(2,1)S(1)} %copy.86), channel_id=1, replica_groups=mesh['strip'=8,'chan'=4] {'chan'}, dimensions={0}, use_global_device_ids=true | all-gather | bytes 983040 | tf_op jit(solution)/shard_map/all_gather | solution.py:95
  98.5 1.4 copy.87
  99.9 0.6 fusion.63
  102.8 1.8 fusion
  104.6 2.6 copy.108
  107.3 0.8 bitcast_dynamic-update-slice_fusion.8
  108.0 0.8 bitcast_dynamic-update-slice_fusion.7
  108.8 0.8 bitcast_dynamic-update-slice_fusion.6
  109.6 0.8 bitcast_dynamic-update-slice_fusion.5
  110.4 0.8 bitcast_dynamic-update-slice_fusion.4
  111.1 0.8 bitcast_dynamic-update-slice_fusion.3
  111.9 0.8 bitcast_dynamic-update-slice_fusion.2
  112.7 0.8 bitcast_dynamic-update-slice_fusion.1
  113.5 0.8 bitcast_dynamic-update-slice_fusion
  114.3 3.1 copy.109
  117.4 2.5 fusion.73
  119.9 4.0 %fusion.74 = f32[128,3,3,512]{3,0,2,1:T(8,128)} fusion(bf16[128,3,3,768]{0,3,2,1:T(8,128)(2,1)} %bitcast.64, bf16[512,768,1,1]{0,1,3,2:T(8,128)(2,1)S(1)} %bitcast.249), kind=kOutput, calls=%fused_computation.146 | convolution fusion | flops 905969664 | bytes 4915200 | tf_op jit(solution)/shard_map/dot_general | solution.py:78
  123.9 2.8 convolution_bitcast_fusion
  126.7 3.0 copy.89
  129.7 4.9 %reshape.55 = f32[128,3,3,6,128]{4,3,2,1,0:T(8,128)} reshape(f32[1152,768]{1,0:T(8,128)} %copy.89) | data formatting | bytes 7077888 | tf_op jit(solution)/shard_map/reshape | solution.py:41
  134.6 2.3 slice_bitcast_fusion.8
  137.8 2.6 fusion.23
  140.4 3.9 %all-reduce.51.cloned.1.call-done = f32[512,4,128]{2,1,0:T(4,128)} async-done(((f32[512,4,128]{2,1,0:T(4,128)}), f32[512,4,128]{2,1,0:T(4,128)}) %all-reduce.51.cloned.1.call-update) | async-done | bytes 1048592
  144.2 1.7 fusion.38
  145.9 172.9 %all-reduce.53.cloned.1.call-done = (f32[128,3,3,512]{3,0,2,1:T(8,128)}, f32[128,3,3,512]{3,0,2,1:T(8,128)}) async-done(((f32[128,3,3,512]{3,0,2,1:T(8,128)}, f32[128,3,3,512]{3,0,2,1:T(8,128)}), (f32[128,3,3,512]{3,0,2,1:T(8,128)}, f32[128,3,3,512]{3,0,2,1:T(8,128)})) %all-reduce.53.cloned.1.call-update) | async-done | bytes 4718608 | tf_op jit(solution)/shard_map/psum | solution.py:120
  318.9 3.4 %copy.185 = f32[128,3,3,512]{3,0,2,1:T(8,128)} copy(f32[128,3,3,512]{3,0,2,1:T(8,128)} %get-tuple-element.38) | data formatting | bytes 4718592
  322.3 1.4 copy.186
  (63 shorter events, 4.4 us)
Async XLA Ops:
  7.2 68.2 %all-reduce.49.cloned.1.call-start = ((), (), s32[]{:S(2)}) async-start(), calls=%async_computation | async-start | bytes 2097152
  8.3 23.2 %collective-permute-start.5 = (bf16[128,1,128]{0,2,1:T(8,128)(2,1)S(1)}, bf16[128,1,128]{0,2,1:T(8,128)(2,1)S(1)}, u32[]{:S(2)}, u32[]{:S(2)}) collective-permute-start(bf16[128,1,128]{0,2,1:T(8,128)(2,1)S(1)} %get-tuple-element.34), channel_id=1, source_target_pairs={{0,4},{4,8},{8,12},{12,16},{16,20},{20,24},{24,28},{1,5},{5,9},{9,... | collective-permute-start | bytes 98312 | tf_op jit(solution)/shard_map/ppermute | solution.py:15
  13.1 18.4 %collective-permute-start.4 = (bf16[128,1,128]{0,2,1:T(8,128)(2,1)S(1)}, bf16[128,1,128]{0,2,1:T(8,128)(2,1)S(1)}, u32[]{:S(2)}, u32[]{:S(2)}) collective-permute-start(bf16[128,1,128]{0,2,1:T(8,128)(2,1)S(1)} %get-tuple-element.35), channel_id=1, source_target_pairs={{4,0},{8,4},{12,8},{16,12},{20,16},{24,20},{28,24},{5,1},{9,5},{13... | collective-permute-start | bytes 98312 | tf_op jit(solution)/shard_map/ppermute | solution.py:17
  15.5 22.0 %collective-permute-start.1 = (bf16[128,1,128]{0,2,1:T(8,128)(2,1)S(1)}, bf16[128,1,128]{0,2,1:T(8,128)(2,1)S(1)}, u32[]{:S(2)}, u32[]{:S(2)}) collective-permute-start(bf16[128,1,128]{0,2,1:T(8,128)(2,1)S(1)} %get-tuple-element.29), channel_id=1, source_target_pairs={{4,0},{8,4},{12,8},{16,12},{20,16},{24,20},{28,24},{5,1},{9,5},{13... | collective-permute-start | bytes 98312 | tf_op jit(solution)/shard_map/ppermute | solution.py:17
  16.8 20.7 %collective-permute-start = (bf16[128,1,128]{0,2,1:T(8,128)(2,1)S(1)}, bf16[128,1,128]{0,2,1:T(8,128)(2,1)S(1)}, u32[]{:S(2)}, u32[]{:S(2)}) collective-permute-start(bf16[128,1,128]{0,2,1:T(8,128)(2,1)S(1)} %get-tuple-element.28), channel_id=1, source_target_pairs={{0,4},{4,8},{8,12},{12,16},{16,20},{20,24},{24,28},{1,5},{5,9},{9,... | collective-permute-start | bytes 98312 | tf_op jit(solution)/shard_map/ppermute | solution.py:15
  25.3 8.6 %copy-start.1 = (bf16[1152,512]{1,0:T(8,128)(2,1)}, bf16[1152,512]{1,0:T(8,128)(2,1)S(1)}, u32[]{:S(2)}) copy-start(bf16[1152,512]{1,0:T(8,128)(2,1)S(1)} %reshape.54) | copy-start | bytes 3538948
  28.0 2.2 copy-start.6
  37.4 8.9 %copy-start.2 = (bf16[1152,512]{1,0:T(8,128)(2,1)S(1)}, bf16[1152,512]{1,0:T(8,128)(2,1)}, u32[]{:S(2)}) copy-start(bf16[1152,512]{1,0:T(8,128)(2,1)} %reshape.51) | copy-start | bytes 3538948
  37.4 106.8 %all-reduce.51.cloned.1.call-start = ((), (), s32[]{:S(2)}) async-start(), calls=%async_computation.1 | async-start | bytes 2097152
  78.0 11.5 %collective-permute-start.3 = (bf16[128,1,128]{2,1,0:T(2,128)(2,1)S(1)}, bf16[128,1,128]{2,1,0:T(2,128)(2,1)S(1)}, u32[]{:S(2)}, u32[]{:S(2)}) collective-permute-start(bf16[128,1,128]{2,1,0:T(2,128)(2,1)S(1)} %get-tuple-element.27), channel_id=1, source_target_pairs={{4,0},{8,4},{12,8},{16,12},{20,16},{24,20},{28,24},{5,1},{9,5},{13... | collective-permute-start | bytes 98312 | tf_op jit(solution)/shard_map/ppermute | solution.py:17
  79.3 10.3 %collective-permute-start.2 = (bf16[128,1,128]{2,1,0:T(2,128)(2,1)S(1)}, bf16[128,1,128]{2,1,0:T(2,128)(2,1)S(1)}, u32[]{:S(2)}, u32[]{:S(2)}) collective-permute-start(bf16[128,1,128]{2,1,0:T(2,128)(2,1)S(1)} %get-tuple-element.26), channel_id=1, source_target_pairs={{0,4},{4,8},{8,12},{12,16},{16,20},{20,24},{24,28},{1,5},{5,9},{9,... | collective-permute-start | bytes 98312 | tf_op jit(solution)/shard_map/ppermute | solution.py:15
  83.9 16.0 %collective-permute-start.7 = (bf16[128,1,128]{2,1,0:T(2,128)(2,1)S(1)}, bf16[128,1,128]{2,1,0:T(2,128)(2,1)S(1)}, u32[]{:S(2)}, u32[]{:S(2)}) collective-permute-start(bf16[128,1,128]{2,1,0:T(2,128)(2,1)S(1)} %get-tuple-element.24), channel_id=1, source_target_pairs={{0,4},{4,8},{8,12},{12,16},{16,20},{20,24},{24,28},{1,5},{5,9},{9,... | collective-permute-start | bytes 98312 | tf_op jit(solution)/shard_map/ppermute | solution.py:15
  88.2 11.7 %collective-permute-start.6 = (bf16[128,1,128]{2,1,0:T(2,128)(2,1)S(1)}, bf16[128,1,128]{2,1,0:T(2,128)(2,1)S(1)}, u32[]{:S(2)}, u32[]{:S(2)}) collective-permute-start(bf16[128,1,128]{2,1,0:T(2,128)(2,1)S(1)} %get-tuple-element.25), channel_id=1, source_target_pairs={{4,0},{8,4},{12,8},{16,12},{20,16},{24,20},{28,24},{5,1},{9,5},{13... | collective-permute-start | bytes 98312 | tf_op jit(solution)/shard_map/ppermute | solution.py:17
  99.9 20.0 %copy-start = (bf16[512,6,128]{0,2,1:T(8,128)(2,1)}, bf16[512,6,128]{0,2,1:T(8,128)(2,1)S(1)}, u32[]{:S(2)}) copy-start(bf16[512,6,128]{0,2,1:T(8,128)(2,1)S(1)} %copy.87) | copy-start | bytes 2359300
  107.2 211.6 %all-reduce.53.cloned.1.call-start = ((), (), s32[]{:S(2)}) async-start(), calls=%async_computation.2 | async-start | bytes 9437184 | tf_op jit(solution)/shard_map/psum | solution.py:120
  136.9 0.9 copy-start.4
  137.3 6.9 %copy-start.5 = (bf16[128,4,128]{2,1,0:T(4,128)(2,1)S(1)}, bf16[128,4,128]{2,1,0:T(4,128)(2,1)}, u32[]{:S(2)}) copy-start(bf16[128,4,128]{2,1,0:T(4,128)(2,1)} %param.7) | copy-start | bytes 393220
  318.9 3.4 %copy-start.3 = (f32[128,3,3,512]{3,0,2,1:T(8,128)S(1)}, f32[128,3,3,512]{3,0,2,1:T(8,128)}, u32[]{:S(2)}) copy-start(f32[128,3,3,512]{3,0,2,1:T(8,128)} %get-tuple-element.39) | copy-start | bytes 7077892
Sparse Core Ops, SparseCore 0:
  37.6 37.7 all-reduce.48
  107.3 36.8 all-reduce.50
  148.5 170.3 all-reduce.52
where the time goes:
time: 331 us; the launch traced here: 330 us
  waiting for transfers between devices  182 us (55%)
  local copies, waits for them, and re-layouts  67.1 us (20%)
  starting transfers between devices  24.1 us (7%)
  blocking collectives  17.4 us (5%)
  matrix products  16.2 us (5%)
  between operations  14.8 us (4%)
  other arithmetic  8.83 us (3%)
    psum x1, waiting for transfers between devices, body(): first_grad = lax.psum(first_grad, 'strip')  173 us
    unnamed x47, local copies, waits for them, and re-layouts  25.3 us
    ppermute x4, starting transfers between devices, extended(): lax.ppermute(tail, axis, [(i, (i + 1) % count) for i in range(ends)])  18.8 us
    reshape x2, local copies, waits for them, and re-layouts, conv_fwd(): taps = taps.reshape(outs, 3, 3, rows_pad, cols)  9.68 us
    all_gather x1, blocking collectives, body(): x_all = lax.all_gather(x_pad, 'chan', axis=0, tiled=True)  8.77 us
    all_gather x1, blocking collectives, body(): h_all = lax.all_gather(h_pad, 'chan', axis=0, tiled=True)  8.68 us
    unnamed x5, waiting for transfers between devices  8.64 us
    dot_general x2, local copies, waits for them, and re-layouts, conv_fwd(): jnp.dot(flat_w, padded.reshape(chans, rows_pad * cols), preferred_element...  8.27 us
  transfers between devices with their start and end apart: 11, of which 3 were waited for; matrix products, arithmetic and copies ran while one was open for 23% of the time, Pallas kernels for 0%

commit v1 on v0

--- a/solution.py
+++ b/solution.py
@@ -85,6 +85,11 @@
 
 
 def body(features, first_filters, second_filters, out_grad):
+
+    def supply_weights(mine):
+        mixed_arr = jnp.sum(lax.all_gather(mine, "strip"), axis=0)
+        return mixed_arr
+
     blocks, rows, cols = features.shape
     x_pad = extended(features, (("strip", 1),), 1)
     x_all = lax.all_gather(x_pad, "chan", axis=0, tiled=True)
@@ -117,7 +122,7 @@
         tiled=True,
     )
     input_grad = (out_grad.astype(jnp.float32) + input_term).astype(jnp.bfloat16)
-    first_grad = lax.psum(first_grad, "strip")
+    first_grad = supply_weights(first_grad)
     return (output, input_grad, first_grad, second_grad)
 
 

time: 331 us -> 623 us (1.88)
  waiting for transfers between devices: 182 us -> 464 us
  other arithmetic: 8.83 us -> 20 us
    all_gather x0 -> x1, waiting for transfers between devices: none -> 346 us  [supply_weights(): mixed_arr = jnp.sum(lax.all_gather(mine, 'strip'), axis=0)]
    psum x1, waiting for transfers between devices: 173 us -> 102 us  [body(): second_grad = lax.psum(second_grad, 'strip')]
    reduce_sum x0 -> x1, other arithmetic: none -> 10.4 us  [supply_weights(): mixed_arr = jnp.sum(lax.all_gather(mine, 'strip'), axis=0)]
    unnamed x47 -> x46, local copies, waits for them, and re-layouts: 25.3 us -> 20.1 us
  transfers between devices with their start and end apart: 11 -> 12, of which waited for: 3 -> 7; matrix products, arithmetic and copies ran while one was open for 23% -> 13% of each run, Pallas kernels for 0% -> 0%
where the time goes in v1:
time: 623 us; the launch traced here: 622 us
  waiting for transfers between devices  464 us (74%)
  local copies, waits for them, and re-layouts  63.1 us (10%)
  starting transfers between devices  23.8 us (4%)
  blocking collectives  20.4 us (3%)
  other arithmetic  20 us (3%)
  matrix products  15 us (2%)
  between operations  14.8 us (2%)
    all_gather x1, waiting for transfers between devices, supply_weights(): mixed_arr = jnp.sum(lax.all_gather(mine, 'strip'), axis=0)  346 us
    psum x1, waiting for transfers between devices, body(): second_grad = lax.psum(second_grad, 'strip')  102 us
    unnamed x46, local copies, waits for them, and re-layouts  20.1 us
    ppermute x4, starting transfers between devices, extended(): lax.ppermute(tail, axis, [(i, (i + 1) % count) for i in range(ends)])  18.3 us
  transfers between devices with their start and end apart: 12, of which 7 were waited for; matrix products, arithmetic and copies ran while one was open for 13% of the time, Pallas kernels for 0%

profile of v1, /device:TPU:0, one launch (start us, length us, event | category | flops | bytes accessed | tf_op | source)
XLA Modules:
  0.0 621.7 jit_solution(15764292050677626648)
XLA Ops:
  7.2 1.0 copy.99
  8.3 4.8 collective-permute-start.5
  13.1 1.3 collective-permute-start.4
  14.4 1.0 copy.72
  15.5 1.3 collective-permute-start.1
  16.8 5.2 collective-permute-start
  22.0 2.3 copy.88
  24.3 1.1 reshape.58
  25.3 2.7 copy.75
  28.1 2.2 reshape.55
  30.3 0.6 dynamic-slice
  31.9 2.0 copy.105
  33.9 2.1 fusion.3
  36.0 1.3 copy.106
  37.5 8.8 %all_gather.9 = bf16[512,6,128]{0,2,1:T(8,128)(2,1)S(1)} all-gather(bf16[128,6,128]{0,2,1:T(8,128)(2,1)S(1)} %pad_maximum_fusion.1), channel_id=1, replica_groups=mesh['strip'=8,'chan'=4] {'chan'}, dimensions={0}, use_global_device_ids=true | all-gather | bytes 983040 | tf_op jit(solution)/shard_map/all_gather | solution.py:95
  46.3 3.0 convolution_bitcast_fusion.1
  49.2 5.2 copy.76
  54.5 4.8 reshape.56
  59.3 3.0 slice_bitcast_fusion.17
  62.3 0.9 slice.264
  63.2 0.9 slice.259
  64.1 0.9 slice.254
  65.0 10.3 %all-reduce.50.cloned.1.call-done = f32[512,4,128]{2,1,0:T(4,128)} async-done(((f32[512,4,128]{2,1,0:T(4,128)}), f32[512,4,128]{2,1,0:T(4,128)}) %all-reduce.50.cloned.1.call-update) | async-done | bytes 1048592
  75.3 3.0 fusion.11
  78.5 3.4 collective-permute-start.7
  81.9 1.3 collective-permute-start.6
  83.2 0.6 collective-permute-done.7
  83.7 4.3 collective-permute-done.6
  88.0 0.6 fusion.63
  88.9 0.4 fusion.56
  90.1 0.4 fusion.59
  90.5 0.4 copy.107
  90.9 1.8 fusion
  92.7 2.5 copy.108
  95.5 0.8 bitcast_dynamic-update-slice_fusion.8
  96.3 0.8 bitcast_dynamic-update-slice_fusion.7
  97.0 0.8 bitcast_dynamic-update-slice_fusion.6
  97.8 0.8 bitcast_dynamic-update-slice_fusion.5
  98.6 0.8 bitcast_dynamic-update-slice_fusion.4
  99.4 0.8 bitcast_dynamic-update-slice_fusion.3
  100.2 0.8 bitcast_dynamic-update-slice_fusion.2
  101.0 0.8 bitcast_dynamic-update-slice_fusion.1
  101.8 0.8 bitcast_dynamic-update-slice_fusion
  102.5 3.1 copy.109
  105.6 2.5 fusion.73
  108.6 0.5 copy-done.3
  109.4 1.3 collective-permute-start.3
  110.7 4.9 collective-permute-start.2
  115.9 1.6 collective-permute-done.2
  117.8 11.7 %all_gather.10 = bf16[512,6,128]{2,0,1:T(8,128)(2,1)S(1)} all-gather(bf16[128,6,128]{2,0,1:T(8,128)(2,1)S(1)} %copy.86), channel_id=1, replica_groups=mesh['strip'=8,'chan'=4] {'chan'}, dimensions={0}, use_global_device_ids=true | all-gather | bytes 983040 | tf_op jit(solution)/shard_map/all_gather | solution.py:100
  129.4 0.3 copy.87
  129.7 2.5 fusion.74
  132.3 1.2 copy-done.1
  133.5 3.0 convolution_bitcast_fusion
  136.5 5.2 copy.89
  141.7 4.9 reshape.59
  146.6 2.3 slice_bitcast_fusion.8
  149.6 0.3 copy-done.4
  149.8 2.6 fusion.23
  152.4 1.7 fusion.38
  154.1 345.6 %all-gather.3.cloned.1.call-done = f32[1024,3,3,512]{3,0,2,1:T(8,128)} async-done(((f32[128,3,3,512]{3,0,2,1:T(8,128)}), f32[1024,3,3,512]{3,0,2,1:T(8,128)}) %all-gather.3.cloned.1.call-update) | async-done | bytes 18874384 | tf_op jit(solution)/shard_map/all_gather | solution.py:90
  499.7 10.4 %reduce_sum.9 = f32[128,3,3,512]{3,0,2,1:T(8,128)} reduce(f32[8,128,3,3,512]{4,1,0,3,2:T(8,128)} %bitcast.247, f32[]{:T(128)} %constant.3.clone.1), dimensions={0}, to_apply=%region_2.3 | reduce | flops 4128768 | bytes 21233668 | tf_op jit(solution)/shard_map/reduce_sum | solution.py:90
  510.1 101.8 %all-reduce.48.cloned.1.call-done = f32[128,3,3,512]{3,0,2,1:T(8,128)} async-done(((f32[128,3,3,512]{3,0,2,1:T(8,128)}), f32[128,3,3,512]{3,0,2,1:T(8,128)}) %all-reduce.48.cloned.1.call-update) | async-done | bytes 2359312 | tf_op jit(solution)/shard_map/psum | solution.py:104
  611.9 3.3 copy.184
  (66 shorter events, 3.8 us)
Async XLA Ops:
  7.2 68.2 %all-reduce.50.cloned.1.call-start = ((), (), s32[]{:S(2)}) async-start(), calls=%async_computation.2 | async-start | bytes 2097152
  8.3 23.2 %collective-permute-start.5 = (bf16[128,1,128]{0,2,1:T(8,128)(2,1)S(1)}, bf16[128,1,128]{0,2,1:T(8,128)(2,1)S(1)}, u32[]{:S(2)}, u32[]{:S(2)}) collective-permute-start(bf16[128,1,128]{0,2,1:T(8,128)(2,1)S(1)} %get-tuple-element.32), channel_id=1, source_target_pairs={{0,4},{4,8},{8,12},{12,16},{16,20},{20,24},{24,28},{1,5},{5,9},{9,... | collective-permute-start | bytes 98312 | tf_op jit(solution)/shard_map/ppermute | solution.py:15
  13.1 18.4 %collective-permute-start.4 = (bf16[128,1,128]{0,2,1:T(8,128)(2,1)S(1)}, bf16[128,1,128]{0,2,1:T(8,128)(2,1)S(1)}, u32[]{:S(2)}, u32[]{:S(2)}) collective-permute-start(bf16[128,1,128]{0,2,1:T(8,128)(2,1)S(1)} %get-tuple-element.33), channel_id=1, source_target_pairs={{4,0},{8,4},{12,8},{16,12},{20,16},{24,20},{28,24},{5,1},{9,5},{13... | collective-permute-start | bytes 98312 | tf_op jit(solution)/shard_map/ppermute | solution.py:17
  15.5 22.0 %collective-permute-start.1 = (bf16[128,1,128]{0,2,1:T(8,128)(2,1)S(1)}, bf16[128,1,128]{0,2,1:T(8,128)(2,1)S(1)}, u32[]{:S(2)}, u32[]{:S(2)}) collective-permute-start(bf16[128,1,128]{0,2,1:T(8,128)(2,1)S(1)} %get-tuple-element.27), channel_id=1, source_target_pairs={{4,0},{8,4},{12,8},{16,12},{20,16},{24,20},{28,24},{5,1},{9,5},{13... | collective-permute-start | bytes 98312 | tf_op jit(solution)/shard_map/ppermute | solution.py:17
  16.8 20.7 %collective-permute-start = (bf16[128,1,128]{0,2,1:T(8,128)(2,1)S(1)}, bf16[128,1,128]{0,2,1:T(8,128)(2,1)S(1)}, u32[]{:S(2)}, u32[]{:S(2)}) collective-permute-start(bf16[128,1,128]{0,2,1:T(8,128)(2,1)S(1)} %get-tuple-element.26), channel_id=1, source_target_pairs={{0,4},{4,8},{8,12},{12,16},{16,20},{20,24},{24,28},{1,5},{5,9},{9,... | collective-permute-start | bytes 98312 | tf_op jit(solution)/shard_map/ppermute | solution.py:15
  25.3 8.6 %copy-start = (bf16[1152,512]{1,0:T(8,128)(2,1)}, bf16[1152,512]{1,0:T(8,128)(2,1)S(1)}, u32[]{:S(2)}) copy-start(bf16[1152,512]{1,0:T(8,128)(2,1)S(1)} %reshape.58) | copy-start | bytes 3538948
  28.0 2.2 copy-start.6
  37.3 8.9 %copy-start.2 = (bf16[1152,512]{1,0:T(8,128)(2,1)S(1)}, bf16[1152,512]{1,0:T(8,128)(2,1)}, u32[]{:S(2)}) copy-start(bf16[1152,512]{1,0:T(8,128)(2,1)} %reshape.55) | copy-start | bytes 3538948
  37.4 115.0 %all-reduce.52.cloned.1.call-start = ((), (), s32[]{:S(2)}) async-start(), calls=%async_computation.3 | async-start | bytes 2097152
  78.5 5.3 collective-permute-start.7
  81.9 6.2 collective-permute-start.6
  95.3 404.4 %all-gather.3.cloned.1.call-start = ((), (), s32[]{:S(2)}) async-start(), calls=%async_computation.1 | async-start | bytes 21233664 | tf_op jit(solution)/shard_map/all_gather | solution.py:90
  108.2 1.0 copy-start.3
  108.2 503.7 %all-reduce.48.cloned.1.call-start = ((), (), s32[]{:S(2)}) async-start(), calls=%async_computation | async-start | bytes 4718592 | tf_op jit(solution)/shard_map/psum | solution.py:104
  109.4 6.5 %collective-permute-start.3 = (bf16[128,1,128]{2,1,0:T(2,128)(2,1)S(1)}, bf16[128,1,128]{2,1,0:T(2,128)(2,1)S(1)}, u32[]{:S(2)}, u32[]{:S(2)}) collective-permute-start(bf16[128,1,128]{2,1,0:T(2,128)(2,1)S(1)} %get-tuple-element.25), channel_id=1, source_target_pairs={{4,0},{8,4},{12,8},{16,12},{20,16},{24,20},{28,24},{5,1},{9,5},{13... | collective-permute-start | bytes 98312 | tf_op jit(solution)/shard_map/ppermute | solution.py:17
  110.7 6.8 %collective-permute-start.2 = (bf16[128,1,128]{2,1,0:T(2,128)(2,1)S(1)}, bf16[128,1,128]{2,1,0:T(2,128)(2,1)S(1)}, u32[]{:S(2)}, u32[]{:S(2)}) collective-permute-start(bf16[128,1,128]{2,1,0:T(2,128)(2,1)S(1)} %get-tuple-element.24), channel_id=1, source_target_pairs={{0,4},{4,8},{8,12},{12,16},{16,20},{20,24},{24,28},{1,5},{5,9},{9,... | collective-permute-start | bytes 98312 | tf_op jit(solution)/shard_map/ppermute | solution.py:15
  132.2 1.3 copy-start.1
  148.9 0.9 copy-start.4
  149.3 3.1 copy-start.5
Sparse Core Ops, SparseCore 0:
  37.5 37.7 all-reduce.49
  95.4 38.7 all-reduce.51
  136.3 363.3 all-gather.2
  503.1 108.6 all-reduce.47
